TPU v7x, 256 devices: a whole 4x4x8 slice. The times are simulated.
256 devices in a mesh: req: 32 (over x, y, core), tp: 8 (over z).
Axes of the slice: x: 4, y: 4, z: 8, core: 2. Of those that a mesh axis runs over, the one named last changes fastest.
Arguments:
- query: bfloat16 [768, 4096], P('req', 'tp'), may hold values from -102 to 102
- new_key: bfloat16 [768, 1024], P('req', 'tp'), may hold values from -6 to 6
- new_value: bfloat16 [768, 1024], P('req', 'tp'), may hold values from -6 to 6
- prefix_key: bfloat16 [64, 6144, 1024], P('req', None, 'tp'), may hold values from -6 to 6
- prefix_value: bfloat16 [64, 6144, 1024], P('req', None, 'tp'), may hold values from -6 to 6
- suffix_key: bfloat16 [768, 128, 1024], P('req', None, 'tp'), may hold values from -6 to 6
- suffix_value: bfloat16 [768, 128, 1024], P('req', None, 'tp'), may hold values from -6 to 6
- group_ids: int32 [768], replicated, may hold values from 0 to 63, as said below
- prompt_len: int32 [64], P('req'), may hold values from 768 to 6144, as said below
- suffix_len: int32 [768], replicated, may hold values from 1 to 128, as said below
- o_weight: bfloat16 [4096, 4096], P('tp'), may hold values from -0.09375 to 0.09375
- residual: bfloat16 [768, 4096], P('req'), may hold values from -0.29882812 to 0.29882812
- norm_gain: bfloat16 [4096], replicated, may hold values from 0.5 to 1.5
Outputs:
- hidden: bfloat16 [768, 4096], P('req')
- normed: bfloat16 [768, 4096], P('req')
Inputs may be any that keep to these rules, and one draw needn't show every extreme that they name: Request r belongs to group group_ids[r]; groups 2k to 2k + 1 at a time are held together (group // 2 names the holder). Among each aligned block of 24 requests, every holder that appears is named by exactly 2 of them. `prompt_len`: some group has exactly 6144. `suffix_len`: some request has exactly 128.
All inputs are finite; a program needn't handle non-finite values.
Results may differ from a plain program's by a relative error of at most 0.008.
Values may be sent and summed in bfloat16 or wider, within the bound.
No kernel may reach another device: no remote copies, remote signals or barrier semaphores. Data moves between devices by JAX's collectives and lax.ppermute only.
A program may use at most 64 MiB of HBM per device.

v0:
```python
import math
import jax
import jax.numpy as jnp
from jax import lax
from jax.sharding import PartitionSpec as P

HD = 128
WIN = 4096
SINKS = 4
FAR_BELOW = -1e30
NORM_EPS = 1e-06


def prefix_attend(
    rows_query, row_group, row_suffix, prefix_key, prefix_value, prompt_len, first_group, blocks
):
    row_count = rows_query.shape[0]
    groups_dev = prefix_key.shape[0]
    prompt_max = prefix_key.shape[1]
    kv_dev = prefix_key.shape[2] // HD
    heads_dev = rows_query.shape[1] // HD
    repeat = heads_dev // kv_dev
    block_len = min(512, prompt_max)
    score_scale = 1.0 / math.sqrt(HD)
    local_group = row_group - first_group
    owned = (local_group >= 0) & (local_group < groups_dev)
    member = local_group[:, None] == jnp.arange(groups_dev, dtype=jnp.int32)[None, :]
    row_prompt = jnp.sum(jnp.where(member, prompt_len[None, :], 0), axis=1)
    row_low = row_prompt + row_suffix - WIN + 1
    queries = rows_query.reshape(row_count, kv_dev, repeat, HD)

    def key_step(block_index, loop_state):
        running, weight_sum, weighted = loop_state
        key_start = block_index * block_len
        key_block = lax.dynamic_slice_in_dim(prefix_key, key_start, block_len, 1).reshape(
            groups_dev, block_len, kv_dev, HD
        )
        value_block = lax.dynamic_slice_in_dim(prefix_value, key_start, block_len, 1).reshape(
            groups_dev, block_len, kv_dev, HD
        )
        scores = (
            jnp.einsum("rkhd,gpkd->rkhgp", queries, key_block, preferred_element_type=jnp.float32)
            * score_scale
        )
        positions = key_start + jnp.arange(block_len, dtype=jnp.int32)
        inside = positions[None, :] < prompt_len[:, None]
        window = (positions[None, :] < SINKS) | (positions[None, :] >= row_low[:, None])
        usable = member[:, :, None] & inside[None, :, :] & window[:, None, :]
        usable = usable[:, None, None, :, :]
        masked = jnp.where(usable, scores, FAR_BELOW)
        updated = jnp.maximum(running, jnp.max(masked, axis=(3, 4)))
        weights = jnp.where(usable, jnp.exp(masked - updated[..., None, None]), 0.0)
        rescale = jnp.exp(running - updated)
        weight_sum = weight_sum * rescale + jnp.sum(weights, axis=(3, 4))
        rounded = weights.astype(jnp.bfloat16)
        weighted = weighted * rescale[..., None] + jnp.einsum(
            "rkhgp,gpkd->rkhd", rounded, value_block, preferred_element_type=jnp.float32
        )
        return (updated, weight_sum, weighted)

    initial = (
        jnp.full((row_count, kv_dev, repeat), FAR_BELOW, jnp.float32),
        jnp.zeros((row_count, kv_dev, repeat), jnp.float32),
        jnp.zeros((row_count, kv_dev, repeat, HD), jnp.float32),
    )
    running, weight_sum, weighted = lax.fori_loop(0, blocks, key_step, initial)
    bounded = jnp.maximum(weight_sum, 1.0)
    normalized = jnp.where(owned[:, None, None, None], weighted / bounded[..., None], 0.0).reshape(
        row_count, heads_dev * HD
    )
    log_total = jnp.where(owned[:, None, None], running + jnp.log(bounded), 0.0).reshape(
        row_count, heads_dev
    )
    return (normalized, log_total)


def body(
    query,
    new_key,
    new_value,
    prefix_key,
    prefix_value,
    suffix_key,
    suffix_value,
    group_ids,
    prompt_len,
    suffix_len,
    o_weight,
    residual,
    norm_gain,
):
    req_dev = query.shape[0]
    heads_dev = query.shape[1] // HD
    kv_dev = new_key.shape[1] // HD
    repeat = heads_dev // kv_dev
    groups_dev = prefix_key.shape[0]
    prompt_max = prefix_key.shape[1]
    suffix_max = suffix_key.shape[1]
    block_len = min(512, prompt_max)
    score_scale = 1.0 / math.sqrt(HD)
    places = lax.axis_size("req")
    device = lax.axis_index("req")
    first_group = device * groups_dev
    own_suffix = lax.dynamic_slice_in_dim(suffix_len, device * req_dev, req_dev)
    blocks = prompt_max // block_len
    capacity = max(2, req_dev // places)
    slot_total = places * capacity
    all_groups = group_ids.reshape(places, 1, req_dev)
    all_suffix = suffix_len.reshape(places, 1, req_dev)
    all_rows = (
        jnp.arange(places, dtype=jnp.int32)[:, None] * req_dev
        + jnp.arange(req_dev, dtype=jnp.int32)[None, :]
    ).reshape(places, 1, req_dev)
    is_mine = (group_ids // groups_dev).reshape(places, req_dev) == device
    slot_order = jnp.cumsum(is_mine.astype(jnp.int32), axis=1) - 1
    slot_pick = is_mine[:, None, :] & (
        slot_order[:, None, :] == jnp.arange(capacity, dtype=jnp.int32)[None, :, None]
    )
    filled = jnp.any(slot_pick, axis=2)
    slot_group = jnp.where(
        filled, jnp.sum(jnp.where(slot_pick, all_groups, 0), axis=2), -1
    ).reshape(slot_total)
    slot_suffix = jnp.sum(jnp.where(slot_pick, all_suffix, 0), axis=2).reshape(slot_total)
    slot_row = jnp.where(filled, jnp.sum(jnp.where(slot_pick, all_rows, 0), axis=2), -1).reshape(
        slot_total
    )
    own_groups = lax.dynamic_slice_in_dim(group_ids, device * req_dev, req_dev)
    own_holder = own_groups // groups_dev
    same_holder = own_holder[:, None] == own_holder[None, :]
    earlier = (
        jnp.arange(req_dev, dtype=jnp.int32)[None, :]
        < jnp.arange(req_dev, dtype=jnp.int32)[:, None]
    )
    own_rank = jnp.sum(same_holder & earlier, axis=1).astype(jnp.int32)
    own_slot = own_holder * capacity + own_rank
    send_pick = own_slot[None, :] == jnp.arange(slot_total, dtype=jnp.int32)[:, None]
    send_query = jnp.dot(
        send_pick.astype(jnp.bfloat16), query, preferred_element_type=jnp.float32
    ).astype(jnp.bfloat16)
    compact = lax.all_to_all(
        send_query.reshape(places, capacity, heads_dev * HD), "req", 0, 0, tiled=True
    ).reshape(slot_total, heads_dev * HD)
    part_out, part_log = prefix_attend(
        compact, slot_group, slot_suffix, prefix_key, prefix_value, prompt_len, first_group, blocks
    )
    packed = jnp.concatenate([part_out, part_log], axis=1)
    returned = lax.all_to_all(
        packed.reshape(places, capacity, packed.shape[1]), "req", 0, 0, tiled=True
    ).reshape(slot_total, packed.shape[1])
    picked = returned[own_slot]
    prefix_out = picked[:, : heads_dev * HD]
    prefix_log = picked[:, heads_dev * HD :]
    queries = query.reshape(req_dev, kv_dev, repeat, HD)
    key_rows = suffix_key.reshape(req_dev, suffix_max, kv_dev, HD)
    value_rows = suffix_value.reshape(req_dev, suffix_max, kv_dev, HD)
    scores = (
        jnp.einsum("rkhd,rjkd->rkhj", queries, key_rows, preferred_element_type=jnp.float32)
        * score_scale
    )
    own_score = (
        jnp.einsum(
            "rkhd,rkd->rkh",
            queries,
            new_key.reshape(req_dev, kv_dev, HD),
            preferred_element_type=jnp.float32,
        )
        * score_scale
    )
    usable = (jnp.arange(suffix_max, dtype=jnp.int32)[None, :] < own_suffix[:, None])[
        :, None, None, :
    ]
    masked = jnp.where(usable, scores, FAR_BELOW)
    running = jnp.maximum(jnp.max(masked, axis=-1), own_score)
    weights = jnp.where(usable, jnp.exp(masked - running[..., None]), 0.0)
    own_weight = jnp.exp(own_score - running)
    weight_sum = jnp.sum(weights, axis=-1) + own_weight
    weighted = jnp.einsum(
        "rkhj,rjkd->rkhd",
        weights.astype(jnp.bfloat16),
        value_rows,
        preferred_element_type=jnp.float32,
    )
    own_rounded = own_weight.astype(jnp.bfloat16).astype(jnp.float32)
    weighted = weighted + own_rounded[..., None] * new_value.reshape(req_dev, kv_dev, 1, HD).astype(
        jnp.float32
    )
    local_out = weighted / weight_sum[..., None]
    local_log = running + jnp.log(weight_sum)
    prefix_out = prefix_out.reshape(req_dev, kv_dev, repeat, HD)
    prefix_log = prefix_log.reshape(req_dev, kv_dev, repeat)
    combined = jnp.logaddexp(prefix_log, local_log)
    attended = (
        prefix_out * jnp.exp(prefix_log - combined)[..., None]
        + local_out * jnp.exp(local_log - combined)[..., None]
    )
    attended = attended.reshape(req_dev, heads_dev * HD).astype(jnp.bfloat16)
    partial_value = jnp.dot(attended, o_weight, preferred_element_type=jnp.float32)
    proj = lax.psum(partial_value, "tp")
    summed = residual.astype(jnp.float32) + proj
    hidden = summed.astype(jnp.bfloat16)
    inverse = lax.rsqrt(jnp.mean(summed * summed, axis=-1, keepdims=True) + NORM_EPS)
    normed = (summed * inverse * norm_gain.astype(jnp.float32)[None, :]).astype(jnp.bfloat16)
    return (hidden, normed)


def solution(mesh):
    placed = (
        P("req", "tp"),
        P("req", "tp"),
        P("req", "tp"),
        P("req", None, "tp"),
        P("req", None, "tp"),
        P("req", None, "tp"),
        P("req", None, "tp"),
        P(),
        P("req"),
        P(),
        P("tp", None),
        P("req", None),
        P(),
    )
    return jax.shard_map(
        body,
        mesh=mesh,
        in_specs=placed,
        out_specs=(P("req", None), P("req", None)),
        check_vma=False,
    )
```

profile of v0, /device:TPU:2, one launch (start us, length us, event | category | flops | bytes accessed | tf_op | source)
XLA Modules:
  0.0 179.4 jit_solution(5152903580054257857)
XLA Ops:
  10.5 7.6 %all-to-all-start = ((bf16[32,2,512]{2,1,0:T(2,128)(2,1)}), bf16[32,2,512]{2,1,0:T(2,128)(2,1)S(1)}, u32[]{:S(2)}, u32[]{:S(2)}) async-start(bf16[32,2,512]{2,1,0:T(2,128)(2,1)} %reshape.348), calls=%async_computation | async-start | bytes 131072 | tf_op jit(solution)/shard_map/all_to_all | solution.py:140
  25.4 50.1 %while.18 = (s32[]{:T(128)}, f32[64,1,4]{0,2,1:T(4,128)S(1)}, f32[64,1,4]{0,2,1:T(4,128)S(1)}, f32[64,1,4,128]{3,0,2,1:T(8,128)S(1)}, s32[2]{0:T(128)}, /*index=...) while((s32[]{:T(128)}, f32[64,1,4]{0,2,1:T(4,128)S(1)}, ...), condition=%wide.region_9.10_spmd.clone, body=%wide.region_6.9_spmd.clone.sunk | while | flops 136876160 | bytes 4351959 | solution.py:66
  27.9 1.4 fusion.71
  30.7 1.4 fusion.68
  32.1 1.4 fusion.71
  34.8 1.4 fusion.68
  36.2 1.4 fusion.71
  39.0 1.4 fusion.68
  40.4 1.4 fusion.71
  43.2 1.4 fusion.68
  44.6 1.4 fusion.71
  47.4 1.4 fusion.68
  48.7 1.4 fusion.71
  52.9 1.4 fusion.71
  57.1 1.4 fusion.71
  61.2 1.4 fusion.71
  65.4 1.4 fusion.71
  69.6 1.4 fusion.71
  73.7 1.4 fusion.71
  76.7 7.4 %all-to-all-start.1 = ((f32[32,2,516]{2,1,0:T(2,128)}), f32[32,2,516]{2,1,0:T(2,128)S(1)}, u32[]{:S(2)}, u32[]{:S(2)}) async-start(f32[32,2,516]{2,1,0:T(2,128)} %pad_maximum_fusion), calls=%async_computation.1 | async-start | bytes 327680 | tf_op jit(solution)/shard_map/all_to_all | solution.py:147
  84.4 6.6 %all-to-all-done.1 = f32[32,2,516]{2,1,0:T(2,128)S(1)} async-done(((f32[32,2,516]{2,1,0:T(2,128)}), f32[32,2,516]{2,1,0:T(2,128)S(1)}, u32[]{:S(2)}, u32[]{:S(2)}) %all-to-all-start.1) | async-done | bytes 132128 | tf_op jit(solution)/shard_map/all_to_all | solution.py:147
  92.2 3.6 %fusion.30 = f32[24,4096]{1,0:T(8,128)} fusion(bf16[512,4096]{1,0:T(8,128)(2,1)} %param.25, bf16[3,8,4,128]{3,2,1,0:T(4,128)(2,1)S(1)} %bitcast.84), kind=kOutput, calls=%fused_computation.52 | convolution fusion | flops 100663296 | bytes 4612096 | tf_op jit(solution)/shard_map/dot_general | solution.py:197
  95.9 73.7 %all-reduce.2.cloned.1.call-done = f32[24,4096]{1,0:T(8,128)} async-done(((f32[24,4096]{1,0:T(8,128)}), f32[24,4096]{1,0:T(8,128)}) %all-reduce.2.cloned.1.call-update) | async-done | bytes 393232 | tf_op jit(solution)/shard_map/psum | solution.py:198
  170.7 1.8 %multiply_convert_fusion = (bf16[24,4096]{1,0:T(8,128)(2,1)}, bf16[24,4096]{1,0:T(8,128)(2,1)}) fusion(f32[4096]{0:T(1024)S(1)} %convert_element_type.66, f32[24]{0:T(128)S(1)} %add_rsqrt_fusion, f32[24,4096]{1,0:T(8,128)} %all-reduce.2.cloned.1.call-done, bf16[24,4096]{1,0:T(8,128)(2,1)S(1)} %copy-done.1), kind=kLoop, calls=%fused_computation.42 | loop fusion | flops 589824 | bytes 999520 | tf_op jit(solution)/shard_map/convert_element_type | solution.py:202
  (196 shorter events, 39.9 us)
Async XLA Ops:
  7.2 17.5 %copy-start = (bf16[24,128,128]{2,1,0:T(8,128)(2,1)S(1)}, bf16[24,128,128]{2,1,0:T(8,128)(2,1)}, u32[]{:S(2)}) copy-start(bf16[24,128,128]{2,1,0:T(8,128)(2,1)} %param.20) | copy-start | bytes 2359300
  10.5 14.8 %all-to-all-start = ((bf16[32,2,512]{2,1,0:T(2,128)(2,1)}), bf16[32,2,512]{2,1,0:T(2,128)(2,1)S(1)}, u32[]{:S(2)}, u32[]{:S(2)}) async-start(bf16[32,2,512]{2,1,0:T(2,128)(2,1)} %reshape.348), calls=%async_computation | async-start | bytes 131072 | tf_op jit(solution)/shard_map/all_to_all | solution.py:140
  25.4 58.8 %copy-start.3 = (bf16[24,128]{1,0:T(8,128)(2,1)S(1)}, bf16[24,128]{1,0:T(8,128)(2,1)}, u32[]{:S(2)}) copy-start(bf16[24,128]{1,0:T(8,128)(2,1)} %param.17) | copy-start | bytes 18436
  25.4 66.4 %copy-start.4 = (bf16[24,128,128]{2,1,0:T(8,128)(2,1)S(1)}, bf16[24,128,128]{2,1,0:T(8,128)(2,1)}, u32[]{:S(2)}) copy-start(bf16[24,128,128]{2,1,0:T(8,128)(2,1)} %param.21) | copy-start | bytes 2359300
  76.7 14.3 %all-to-all-start.1 = ((f32[32,2,516]{2,1,0:T(2,128)}), f32[32,2,516]{2,1,0:T(2,128)S(1)}, u32[]{:S(2)}, u32[]{:S(2)}) async-start(f32[32,2,516]{2,1,0:T(2,128)} %pad_maximum_fusion), calls=%async_computation.1 | async-start | bytes 327680 | tf_op jit(solution)/shard_map/all_to_all | solution.py:147
  84.1 85.5 %all-reduce.2.cloned.1.call-start = ((), (), s32[]{:S(2)}) async-start(), calls=%async_computation.2 | async-start | bytes 786432 | tf_op jit(solution)/shard_map/psum | solution.py:198
  91.8 4.0 %copy-start.2 = (bf16[4096]{0:T(1024)(128)(2,1)S(1)}, bf16[4096]{0:T(1024)(128)(2,1)}, u32[]{:S(2)}) copy-start(bf16[4096]{0:T(1024)(128)(2,1)} %param.27) | copy-start | bytes 24580
  91.8 77.7 %copy-start.1 = (bf16[24,4096]{1,0:T(8,128)(2,1)S(1)}, bf16[24,4096]{1,0:T(8,128)(2,1)}, u32[]{:S(2)}) copy-start(bf16[24,4096]{1,0:T(8,128)(2,1)} %param.26) | copy-start | bytes 589828
Sparse Core Ops, SparseCore 0:
  96.0 73.5 all-reduce.1
where the time goes:
time: 181 us; the launch traced here: 179 us
  waiting for transfers between devices  80.3 us (44%)
  matrix products  39.3 us (22%)
  other arithmetic  23.8 us (13%)
  starting transfers between devices  15 us (8%)
  between operations  14.3 us (8%)
  local copies, waits for them, and re-layouts  5.63 us (3%)
    psum x1, waiting for transfers between devices, body(): proj = lax.psum(partial_value, 'tp')  73.7 us
    dot_general x12, matrix products, key_step(): jnp.einsum('rkhgp,gpkd->rkhd', rounded, value_block, preferred_element_ty...  16.7 us
    dot_general x12, matrix products, key_step(): jnp.einsum('rkhd,gpkd->rkhgp', queries, key_block, preferred_element_type...  16.3 us
    lt x12, other arithmetic, key_step(): inside = positions[None, :] < prompt_len[:, None]  8.84 us
    all_to_all x1, starting transfers between devices, body(): lax.all_to_all(send_query.reshape(places, capacity, heads_dev * HD), 'req...  7.62 us
    all_to_all x1, starting transfers between devices, body(): lax.all_to_all(packed.reshape(places, capacity, packed.shape[1]), 'req',...  7.38 us
    all_to_all x1, waiting for transfers between devices, body(): lax.all_to_all(packed.reshape(places, capacity, packed.shape[1]), 'req',...  6.6 us
    reduce_sum x12, other arithmetic, key_step(): weight_sum = weight_sum * rescale + jnp.sum(weights, axis=(3, 4))  4.33 us
  transfers between devices with their start and end apart: 3, of which 2 were waited for; matrix products, arithmetic and copies ran while one was open for 4% of the time, Pallas kernels for 0%

commit v1 on v0

--- a/solution.py
+++ b/solution.py
@@ -195,7 +195,7 @@
     )
     attended = attended.reshape(req_dev, heads_dev * HD).astype(jnp.bfloat16)
     partial_value = jnp.dot(attended, o_weight, preferred_element_type=jnp.float32)
-    proj = lax.psum(partial_value, "tp")
+    proj = jnp.sum(lax.all_gather(partial_value, "tp"), axis=0)
     summed = residual.astype(jnp.float32) + proj
     hidden = summed.astype(jnp.bfloat16)
     inverse = lax.rsqrt(jnp.mean(summed * summed, axis=-1, keepdims=True) + NORM_EPS)

time: 181 us -> 153 us (0.85)
  waiting for transfers between devices: 80.3 us -> 51.9 us
    psum x1 -> x0, waiting for transfers between devices: 73.7 us -> none  [body(): proj = lax.psum(partial_value, 'tp')]
    all_gather x0 -> x1, waiting for transfers between devices: none -> 45.3 us  [body(): proj = jnp.sum(lax.all_gather(partial_value, 'tp'), axis=0)]
    reduce_sum x0 -> x1, other arithmetic: none -> 2.08 us  [body(): proj = jnp.sum(lax.all_gather(partial_value, 'tp'), axis=0)]
  transfers between devices with their start and end apart: 3 -> 3, of which waited for: 2 -> 2; matrix products, arithmetic and copies ran while one was open for 4% -> 5% of each run, Pallas kernels for 0% -> 0%
where the time goes in v1:
time: 153 us; the launch traced here: 151 us
  waiting for transfers between devices  51.9 us (34%)
  matrix products  39.3 us (26%)
  other arithmetic  23.9 us (16%)
  starting transfers between devices  15 us (10%)
  between operations  14.4 us (9%)
  local copies, waits for them, and re-layouts  5.63 us (4%)
    all_gather x1, waiting for transfers between devices, body(): proj = jnp.sum(lax.all_gather(partial_value, 'tp'), axis=0)  45.3 us
    dot_general x12, matrix products, key_step(): jnp.einsum('rkhgp,gpkd->rkhd', rounded, value_block, preferred_element_ty...  16.7 us
    dot_general x12, matrix products, key_step(): jnp.einsum('rkhd,gpkd->rkhgp', queries, key_block, preferred_element_type...  16.3 us
    lt x12, other arithmetic, key_step(): inside = positions[None, :] < prompt_len[:, None]  8.84 us
    all_to_all x1, starting transfers between devices, body(): lax.all_to_all(send_query.reshape(places, capacity, heads_dev * HD), 'req...  7.62 us
    all_to_all x1, starting transfers between devices, body(): lax.all_to_all(packed.reshape(places, capacity, packed.shape[1]), 'req',...  7.39 us
    all_to_all x1, waiting for transfers between devices, body(): lax.all_to_all(packed.reshape(places, capacity, packed.shape[1]), 'req',...  6.6 us
    reduce_sum x12, other arithmetic, key_step(): weight_sum = weight_sum * rescale + jnp.sum(weights, axis=(3, 4))  4.33 us
  transfers between devices with their start and end apart: 3, of which 2 were waited for; matrix products, arithmetic and copies ran while one was open for 5% of the time, Pallas kernels for 0%

profile of v1, /device:TPU:2, one launch (start us, length us, event | category | flops | bytes accessed | tf_op | source)
XLA Modules:
  0.0 151.1 jit_solution(13632689863993866610)
XLA Ops:
  10.5 7.6 %all-to-all-start = ((bf16[32,2,512]{2,1,0:T(2,128)(2,1)}), bf16[32,2,512]{2,1,0:T(2,128)(2,1)S(1)}, u32[]{:S(2)}, u32[]{:S(2)}) async-start(bf16[32,2,512]{2,1,0:T(2,128)(2,1)} %reshape.348), calls=%async_computation | async-start | bytes 131072 | tf_op jit(solution)/shard_map/all_to_all | solution.py:140
  25.4 50.1 %while.18 = (s32[]{:T(128)}, f32[64,1,4]{0,2,1:T(4,128)S(1)}, f32[64,1,4]{0,2,1:T(4,128)S(1)}, f32[64,1,4,128]{3,0,2,1:T(8,128)S(1)}, s32[2]{0:T(128)}, /*index=...) while((s32[]{:T(128)}, f32[64,1,4]{0,2,1:T(4,128)S(1)}, ...), condition=%wide.region_9.10_spmd.clone, body=%wide.region_6.9_spmd.clone.sunk | while | flops 136876160 | bytes 4351959 | solution.py:66
  26.5 1.4 fusion.68
  27.9 1.4 fusion.71
  30.7 1.4 fusion.68
  32.1 1.4 fusion.71
  36.2 1.4 fusion.71
  39.0 1.4 fusion.68
  40.4 1.4 fusion.71
  44.6 1.4 fusion.71
  48.7 1.4 fusion.71
  51.5 1.4 fusion.68
  52.9 1.4 fusion.71
  57.1 1.4 fusion.71
  61.2 1.4 fusion.71
  64.0 1.4 fusion.68
  65.4 1.4 fusion.71
  69.5 1.4 fusion.71
  73.7 1.4 fusion.71
  76.7 7.4 %all-to-all-start.1 = ((f32[32,2,516]{2,1,0:T(2,128)}), f32[32,2,516]{2,1,0:T(2,128)S(1)}, u32[]{:S(2)}, u32[]{:S(2)}) async-start(f32[32,2,516]{2,1,0:T(2,128)} %pad_maximum_fusion), calls=%async_computation.1 | async-start | bytes 327680 | tf_op jit(solution)/shard_map/all_to_all | solution.py:147
  84.3 6.6 %all-to-all-done.1 = f32[32,2,516]{2,1,0:T(2,128)S(1)} async-done(((f32[32,2,516]{2,1,0:T(2,128)}), f32[32,2,516]{2,1,0:T(2,128)S(1)}, u32[]{:S(2)}, u32[]{:S(2)}) %all-to-all-start.1) | async-done | bytes 132128 | tf_op jit(solution)/shard_map/all_to_all | solution.py:147
  92.2 3.6 %fusion.30 = f32[24,4096]{1,0:T(8,128)} fusion(bf16[512,4096]{1,0:T(8,128)(2,1)} %param.25, bf16[3,8,4,128]{3,2,1,0:T(4,128)(2,1)S(1)} %bitcast.86), kind=kOutput, calls=%fused_computation.52 | convolution fusion | flops 100663296 | bytes 4612096 | tf_op jit(solution)/shard_map/dot_general | solution.py:197
  95.9 45.3 %all-gather.3.cloned.1.call-done = f32[192,4096]{1,0:T(8,128)} async-done(((f32[24,4096]{1,0:T(8,128)}), f32[192,4096]{1,0:T(8,128)}) %all-gather.3.cloned.1.call-update) | async-done | bytes 3145744 | tf_op jit(solution)/shard_map/all_gather | solution.py:198
  141.2 2.1 %reduce_sum.81 = f32[24,4096]{1,0:T(8,128)S(1)} reduce(f32[8,24,4096]{2,1,0:T(8,128)} %bitcast.80, f32[]{:T(128)} %constant.121.clone.1), dimensions={0}, to_apply=%region_12.13 | reduce | flops 688128 | bytes 3538948 | tf_op jit(solution)/shard_map/reduce_sum | solution.py:198
  (197 shorter events, 39.6 us)
Async XLA Ops:
  7.2 17.5 %copy-start = (bf16[24,128,128]{2,1,0:T(8,128)(2,1)S(1)}, bf16[24,128,128]{2,1,0:T(8,128)(2,1)}, u32[]{:S(2)}) copy-start(bf16[24,128,128]{2,1,0:T(8,128)(2,1)} %param.20) | copy-start | bytes 2359300
  10.5 14.8 %all-to-all-start = ((bf16[32,2,512]{2,1,0:T(2,128)(2,1)}), bf16[32,2,512]{2,1,0:T(2,128)(2,1)S(1)}, u32[]{:S(2)}, u32[]{:S(2)}) async-start(bf16[32,2,512]{2,1,0:T(2,128)(2,1)} %reshape.348), calls=%async_computation | async-start | bytes 131072 | tf_op jit(solution)/shard_map/all_to_all | solution.py:140
  25.4 58.7 %copy-start.3 = (bf16[24,128]{1,0:T(8,128)(2,1)S(1)}, bf16[24,128]{1,0:T(8,128)(2,1)}, u32[]{:S(2)}) copy-start(bf16[24,128]{1,0:T(8,128)(2,1)} %param.17) | copy-start | bytes 18436
  25.4 66.4 %copy-start.4 = (bf16[24,128,128]{2,1,0:T(8,128)(2,1)S(1)}, bf16[24,128,128]{2,1,0:T(8,128)(2,1)}, u32[]{:S(2)}) copy-start(bf16[24,128,128]{2,1,0:T(8,128)(2,1)} %param.21) | copy-start | bytes 2359300
  76.7 14.3 %all-to-all-start.1 = ((f32[32,2,516]{2,1,0:T(2,128)}), f32[32,2,516]{2,1,0:T(2,128)S(1)}, u32[]{:S(2)}, u32[]{:S(2)}) async-start(f32[32,2,516]{2,1,0:T(2,128)} %pad_maximum_fusion), calls=%async_computation.1 | async-start | bytes 327680 | tf_op jit(solution)/shard_map/all_to_all | solution.py:147
  84.1 57.1 %all-gather.3.cloned.1.call-start = ((), (), s32[]{:S(2)}) async-start(), calls=%async_computation.2 | async-start | bytes 3538944 | tf_op jit(solution)/shard_map/all_gather | solution.py:198
  91.8 4.1 %copy-start.2 = (bf16[4096]{0:T(1024)(128)(2,1)S(1)}, bf16[4096]{0:T(1024)(128)(2,1)}, u32[]{:S(2)}) copy-start(bf16[4096]{0:T(1024)(128)(2,1)} %param.27) | copy-start | bytes 24580
  92.2 51.1 %copy-start.1 = (bf16[24,4096]{1,0:T(8,128)(2,1)S(1)}, bf16[24,4096]{1,0:T(8,128)(2,1)}, u32[]{:S(2)}) copy-start(bf16[24,4096]{1,0:T(8,128)(2,1)} %param.26) | copy-start | bytes 589828
Sparse Core Ops, SparseCore 0:
  96.0 45.1 all-gather.2
